TPU v7x, 512 devices: a whole 4x4x16 slice. The times are simulated.
512 devices in a mesh: section: 4 (over x), expert: 16 (over z), rep: 8 (over y, core).
Axes of the slice: x: 4, y: 4, z: 16, core: 2. Of those that a mesh axis runs over, the one named last changes fastest.
Arguments:
- tokens: bfloat16 [4, 2048, 4096], P('section', 'expert', 'rep'), may hold values from -6 to 6
- expert_ids: int32 [4, 2048, 2], P('section', 'expert'), may hold values from 0 to 15, all different within a row; in each aligned block of 128 rows (0 to 127, 128 to 255, ..., all dimensions but the last counted through in order) at most 20 rows name the same one
- route_weight: float32 [4, 2048, 2], P('section', 'expert'), may hold values from 0.05 to 0.5
- language: int32 [4, 2048], P('section', 'expert'), may hold values from 0 to 3
- capacity: int32 [4, 16], replicated, may hold values from 0 to 7
- spill_table: int32 [4, 16], P('section'), may hold values from 0 to 15, as said below
- w_gate: bfloat16 [4, 16, 4096, 1024], P('section', 'expert', None, 'rep'), may hold values from -0.09375 to 0.09375
- w_up: bfloat16 [4, 16, 4096, 1024], P('section', 'expert', None, 'rep'), may hold values from -0.09375 to 0.09375
- w_down: bfloat16 [4, 16, 1024, 4096], P('section', 'expert', None, 'rep'), may hold values from -0.1875 to 0.1875
Outputs:
- next_rows: bfloat16 [4, 2048, 4096], P('section', 'expert', 'rep')
Inputs may be any that keep to these rules, and one draw needn't show every extreme that they name: `expert_ids`: each token names 2 different experts. Among the tokens of one index of expert (aligned blocks of 128 rows, sections in order) no expert is named by more than 20 tokens, a bound that some block reaches. `spill_table`: in each section's row every expert names another expert, and every expert is named by exactly one; each row is one cycle through all 16.
All inputs are finite; a program needn't handle non-finite values.
Results may differ from a plain program's by a relative error of at most 0.0057.
Values may be sent and summed in bfloat16 or wider, within the bound.
No kernel may reach another device: no remote copies, remote signals or barrier semaphores. Data moves between devices by JAX's collectives and lax.ppermute only.
A program may use at most 64 MiB of HBM per device.

v0:
```python
import jax
import jax.numpy as jnp
from jax import lax
from jax.sharding import PartitionSpec as P


def passed_along(value, axis, steps):
    count = lax.axis_size(axis)
    pairs = [(source, (source + steps) % count) for source in range(count)]
    return lax.ppermute(value, axis, pairs)


def admission(chosen, language, capacity, experts):
    lang_count = capacity.shape[0]
    hit_table = jnp.sum(
        (chosen[:, :, None] == jnp.arange(experts, dtype=jnp.int32)[None, None, :]).astype(
            jnp.int32
        ),
        axis=1,
    )
    lang_hot = (language[:, None] == jnp.arange(lang_count, dtype=jnp.int32)[None, :]).astype(
        jnp.int32
    )
    lang_hits = lang_hot[:, :, None] * hit_table[:, None, :]
    before = jnp.cumsum(lang_hits, axis=0) - lang_hits
    place_rank = jnp.sum(before * lang_hot[:, :, None], axis=1)
    allowance = jnp.sum(lang_hot[:, :, None] * capacity[None, :, :], axis=1)
    admitted = hit_table * (place_rank < allowance).astype(jnp.int32)
    return (hit_table, admitted)


def slot_sources(markers, slot_table, slot_depth):
    tok_rows = markers.shape[0]
    selected = markers[:, :, None] * (
        slot_table[:, :, None] == jnp.arange(slot_depth, dtype=jnp.int32)[None, None, :]
    ).astype(jnp.int32)
    positions = jnp.arange(tok_rows, dtype=jnp.int32)[:, None, None]
    source = jnp.sum(selected * positions, axis=0)
    filled = jnp.sum(selected, axis=0)
    return jnp.where(filled > 0, source, tok_rows)


def local(tokens, expert_ids, route_weight, language, capacity, spill_table, w_gate, w_up, w_down):
    experts = lax.axis_size("expert")
    chosen = expert_ids[0]
    spill_row = spill_table[0]
    tok_rows, top_count = chosen.shape
    slot_depth = min(tok_rows, max(2, 5 * tok_rows * top_count // (4 * experts)))
    expert_iota = jnp.arange(experts, dtype=jnp.int32)
    hit_table, admitted = admission(chosen, language[0], capacity, experts)
    spilled = hit_table - admitted
    main_slot = jnp.cumsum(admitted, axis=0) - admitted
    spill_slot = jnp.cumsum(spilled, axis=0) - spilled
    spill_move = (spill_row[:, None] == expert_iota[None, :]).astype(jnp.int32)
    spill_marks = jnp.sum(spilled[:, :, None] * spill_move[None, :, :], axis=1)
    spill_places = jnp.sum((spill_slot * spilled)[:, :, None] * spill_move[None, :, :], axis=1)
    row_source = lax.all_gather(tokens[0], "rep", axis=1, tiled=True)
    with_blank = jnp.concatenate(
        [row_source, jnp.zeros((1, row_source.shape[1]), row_source.dtype)], axis=0
    )
    main_source = slot_sources(admitted, main_slot, slot_depth)
    spill_source = slot_sources(spill_marks, spill_places, slot_depth)
    outgoing = jnp.take(with_blank, jnp.stack([main_source, spill_source]), axis=0)
    arrived = jnp.stack(
        [
            lax.all_to_all(outgoing[0], "expert", split_axis=0, concat_axis=0, tiled=True),
            lax.all_to_all(outgoing[1], "expert", split_axis=0, concat_axis=0, tiled=True),
        ]
    )
    feat_width = arrived.shape[3]
    flattened = arrived.reshape(-1, feat_width)
    gate_proj = jnp.dot(flattened, w_gate[0, 0], preferred_element_type=jnp.float32)
    up_proj = jnp.dot(flattened, w_up[0, 0], preferred_element_type=jnp.float32)
    activated = (jax.nn.silu(gate_proj) * up_proj).astype(jnp.bfloat16)
    down_local = w_down[0, 0]
    produced = jnp.dot(
        lax.all_gather(activated, "rep", axis=1, tiled=True),
        down_local,
        preferred_element_type=jnp.float32,
    )
    produced = produced.astype(jnp.bfloat16).reshape(2, experts, slot_depth, down_local.shape[1])
    returned = jnp.stack(
        [
            lax.all_to_all(produced[0], "expert", split_axis=0, concat_axis=0, tiled=True),
            lax.all_to_all(produced[1], "expert", split_axis=0, concat_axis=0, tiled=True),
        ]
    )
    id_match = (chosen[:, :, None] == expert_iota[None, None, :]).astype(jnp.int32)
    row_kept = jnp.sum(id_match * admitted[:, None, :], axis=2)
    row_main = jnp.sum(id_match * main_slot[:, None, :], axis=2)
    row_spill = jnp.sum(id_match * spill_slot[:, None, :], axis=2)
    row_other = jnp.sum(id_match * spill_row[None, None, :], axis=2)
    target = jnp.where(row_kept > 0, chosen, row_other)
    slot_pick = jnp.where(row_kept > 0, row_main, row_spill)
    row_index = (1 - row_kept) * experts * slot_depth + target * slot_depth + slot_pick
    out_width = returned.shape[3]
    picked = jnp.take(returned.reshape(-1, out_width), row_index.reshape(-1), axis=0).reshape(
        tok_rows, top_count, out_width
    )
    combined = jnp.sum(route_weight[0][:, :, None] * picked.astype(jnp.float32), axis=1).astype(
        jnp.bfloat16
    )
    forwarded = passed_along(combined, "section", 1)
    return forwarded[None]


def solution(mesh):
    in_specs = (
        P("section", "expert", "rep"),
        P("section", "expert", None),
        P("section", "expert", None),
        P("section", "expert"),
        P(),
        P("section", None),
        P("section", "expert", None, "rep"),
        P("section", "expert", None, "rep"),
        P("section", "expert", None, "rep"),
    )
    out_specs = P("section", "expert", "rep")
    return jax.shard_map(local, mesh=mesh, in_specs=in_specs, out_specs=out_specs, check_vma=False)
```

profile of v0, /device:TPU:16, one launch (start us, length us, event | category | flops | bytes accessed | tf_op | source)
XLA Modules:
  0.0 496.3 jit_solution(13053874309466298952)
XLA Ops:
  8.8 1.2 multiply_reduce_fusion.1
  13.4 30.4 %all-gather.6.cloned.1.call-done = bf16[1,128,4096]{2,1,0:T(8,128)(2,1)} async-done(((bf16[1,128,512]{2,1,0:T(8,128)(2,1)}), bf16[1,128,4096]{2,1,0:T(8,128)(2,1)}) %all-gather.6.cloned.1.call-update) | async-done | bytes 1048592 | tf_op jit(solution)/shard_map/all_gather | solution.py:57
  43.8 1.3 concatenate.24
  45.1 5.4 %gather_fusion = bf16[640,4096]{1,0:T(8,128)(2,1)} fusion(bf16[129,4096]{1,0:T(8,128)(2,1)S(1)} %concatenate.24, s32[1024]{0:T(1024)S(1)} %pad_clamp_fusion.1), kind=kCustom, calls=%fused_computation | custom fusion | bytes 10488320 | tf_op jit(solution)/shard_map/jit(_take)/gather | solution.py:63
  50.5 7.7 %reshape.378 = bf16[2,16,20,4096]{3,2,1,0:T(8,128)(2,1)} reshape(bf16[640,4096]{1,0:T(8,128)(2,1)} %gather_fusion) | data formatting | bytes 10485760 | tf_op jit(solution)/shard_map/jit(_take)/gather | solution.py:63
  58.2 3.4 broadcast_select_fusion
  62.4 153.6 %all_to_all.20 = bf16[16,20,4096]{2,1,0:T(8,128)(2,1)S(1)} all-to-all(bf16[16,20,4096]{2,1,0:T(8,128)(2,1)S(1)} %get-tuple-element.23), channel_id=1, replica_groups=mesh['section'=4,'expert'=16,'rep'=8] {'expert'}, dimensions={0} | all-to-all | bytes 5242880 | tf_op jit(solution)/shard_map/all_to_all | solution.py:66
  215.9 147.8 %all_to_all.21 = bf16[16,20,4096]{2,1,0:T(8,128)(2,1)S(1)} all-to-all(bf16[16,20,4096]{2,1,0:T(8,128)(2,1)S(1)} %get-tuple-element.24), channel_id=1, replica_groups=mesh['section'=4,'expert'=16,'rep'=8] {'expert'}, dimensions={0} | all-to-all | bytes 5242880 | tf_op jit(solution)/shard_map/all_to_all | solution.py:67
  363.7 3.4 pad_maximum_fusion
  367.1 7.9 %reshape.375 = bf16[640,4096]{1,0:T(8,128)(2,1)} reshape(bf16[2,16,20,4096]{3,2,1,0:T(8,128)(2,1)} %pad_maximum_fusion) | data formatting | bytes 10485760 | tf_op jit(solution)/shard_map/reshape | solution.py:71
  375.0 4.1 fusion.3
  379.3 2.2 fusion
  381.6 27.1 %all-gather.4.cloned.1.call-done = bf16[640,1024]{1,0:T(8,128)(2,1)} async-done(((bf16[640,128]{1,0:T(8,128)(2,1)}), bf16[640,1024]{1,0:T(8,128)(2,1)}) %all-gather.4.cloned.1.call-update) | async-done | bytes 1310736 | tf_op jit(solution)/shard_map/all_gather | solution.py:77
  408.7 2.2 convolution_convert_fusion
  410.9 0.8 squeeze.33
  411.7 12.3 %all-to-all-start.2 = ((bf16[16,20,512]{2,1,0:T(8,128)(2,1)}), bf16[16,20,512]{2,1,0:T(8,128)(2,1)S(1)}, u32[]{:S(2)}, u32[]{:S(2)}) async-start(bf16[16,20,512]{2,1,0:T(8,128)(2,1)} %squeeze.33), calls=%async_computation.2 | async-start | bytes 786432 | tf_op jit(solution)/shard_map/all_to_all | solution.py:84
  424.0 0.8 squeeze.34
  424.8 23.7 %all-to-all-done.2 = bf16[16,20,512]{2,1,0:T(8,128)(2,1)S(1)} async-done(((bf16[16,20,512]{2,1,0:T(8,128)(2,1)}), bf16[16,20,512]{2,1,0:T(8,128)(2,1)S(1)}, u32[]{:S(2)}, u32[]{:S(2)}) %all-to-all-start.2) | async-done | bytes 327712 | tf_op jit(solution)/shard_map/all_to_all | solution.py:84
  448.5 5.7 %all-to-all-start.3 = ((bf16[16,20,512]{2,1,0:T(8,128)(2,1)}), bf16[16,20,512]{2,1,0:T(8,128)(2,1)S(1)}, u32[]{:S(2)}, u32[]{:S(2)}) async-start(bf16[16,20,512]{2,1,0:T(8,128)(2,1)} %squeeze.34), calls=%async_computation.3 | async-start | bytes 786432 | tf_op jit(solution)/shard_map/all_to_all | solution.py:85
  456.2 22.1 %all-to-all-done.3 = bf16[16,20,512]{2,1,0:T(8,128)(2,1)S(1)} async-done(((bf16[16,20,512]{2,1,0:T(8,128)(2,1)}), bf16[16,20,512]{2,1,0:T(8,128)(2,1)S(1)}, u32[]{:S(2)}, u32[]{:S(2)}) %all-to-all-start.3) | async-done | bytes 327712 | tf_op jit(solution)/shard_map/all_to_all | solution.py:85
  478.6 1.2 gather_fusion.1
  479.8 0.9 multiply_reduce_fusion
  480.7 3.4 collective-permute-start
  484.1 4.7 collective-permute-done
  (67 shorter events, 9.5 us)
Async XLA Ops:
  6.5 402.1 %copy-start = (bf16[1,1,1024,512]{3,2,1,0:T(8,128)(2,1)S(1)}, bf16[1,1,1024,512]{3,2,1,0:T(8,128)(2,1)}, u32[]{:S(2)}) copy-start(bf16[1,1,1024,512]{3,2,1,0:T(8,128)(2,1)} %param.17) | copy-start | bytes 3145732
  6.5 37.3 %all-gather.6.cloned.1.call-start = ((), (), s32[]{:S(2)}) async-start(), calls=%async_computation.5 | async-start | bytes 1179648 | tf_op jit(solution)/shard_map/all_gather | solution.py:57
  7.3 401.4 %all-gather.4.cloned.1.call-start = ((), (), s32[]{:S(2)}) async-start(), calls=%async_computation.4 | async-start | bytes 1474560 | tf_op jit(solution)/shard_map/all_gather | solution.py:77
  367.1 7.9 %copy-start.5 = (bf16[1,1,4096,128]{3,2,1,0:T(8,128)(2,1)S(1)}, bf16[1,1,4096,128]{3,2,1,0:T(8,128)(2,1)}, u32[]{:S(2)}) copy-start(bf16[1,1,4096,128]{3,2,1,0:T(8,128)(2,1)} %param.15) | copy-start | bytes 3145732
  375.0 4.2 copy-start.1
  375.0 4.3 copy-start.6
  381.5 72.6 %copy-start.2 = (s32[1,128,2]{1,2,0:T(2,128)S(1)}, s32[1,128,2]{1,2,0:T(2,128)}, u32[]{:S(2)}) copy-start(s32[1,128,2]{1,2,0:T(2,128)} %param.10) | copy-start | bytes 3076
  381.5 72.8 %copy-start.3 = (s32[1,16]{1,0:T(1,128)S(1)}, s32[1,16]{1,0:T(1,128)}, u32[]{:S(2)}) copy-start(s32[1,16]{1,0:T(1,128)} %param.14) | copy-start | bytes 196
  381.5 74.5 %copy-start.4 = (f32[1,128,2]{1,2,0:T(2,128)S(1)}, f32[1,128,2]{1,2,0:T(2,128)}, u32[]{:S(2)}) copy-start(f32[1,128,2]{1,2,0:T(2,128)} %param.11) | copy-start | bytes 3076
  411.7 36.8 %all-to-all-start.2 = ((bf16[16,20,512]{2,1,0:T(8,128)(2,1)}), bf16[16,20,512]{2,1,0:T(8,128)(2,1)S(1)}, u32[]{:S(2)}, u32[]{:S(2)}) async-start(bf16[16,20,512]{2,1,0:T(8,128)(2,1)} %squeeze.33), calls=%async_computation.2 | async-start | bytes 786432 | tf_op jit(solution)/shard_map/all_to_all | solution.py:84
  448.5 29.9 %all-to-all-start.3 = ((bf16[16,20,512]{2,1,0:T(8,128)(2,1)}), bf16[16,20,512]{2,1,0:T(8,128)(2,1)S(1)}, u32[]{:S(2)}, u32[]{:S(2)}) async-start(bf16[16,20,512]{2,1,0:T(8,128)(2,1)} %squeeze.34), calls=%async_computation.3 | async-start | bytes 786432 | tf_op jit(solution)/shard_map/all_to_all | solution.py:85
  480.7 8.1 %collective-permute-start = (bf16[128,512]{1,0:T(8,128)(2,1)S(1)}, bf16[128,512]{1,0:T(8,128)(2,1)S(1)}, u32[]{:S(2)}, u32[]{:S(2)}) collective-permute-start(bf16[128,512]{1,0:T(8,128)(2,1)S(1)} %multiply_reduce_fusion), channel_id=1, source_target_pairs={{0,128},{128,256},{256,384},{384,0},{1,129},{129,257},{257,385},{3... | collective-permute-start | bytes 393224 | tf_op jit(solution)/shard_map/ppermute | solution.py:10
Sparse Core Ops, SparseCore 0:
  9.5 34.2 all-gather.5
  381.7 26.9 all-gather.3
where the time goes:
time: 497 us; the launch traced here: 496 us
  blocking collectives  301 us (61%)
  waiting for transfers between devices  109 us (22%)
  local copies, waits for them, and re-layouts  29.4 us (6%)
  starting transfers between devices  21.4 us (4%)
  between operations  13.6 us (3%)
  other arithmetic  13.3 us (3%)
  matrix products  8.48 us (2%)
    all_to_all x1, blocking collectives, local(): lax.all_to_all(outgoing[0], 'expert', split_axis=0, concat_axis=0, tiled=...  154 us
    all_to_all x1, blocking collectives, local(): lax.all_to_all(outgoing[1], 'expert', split_axis=0, concat_axis=0, tiled=...  148 us
    all_gather x1, waiting for transfers between devices, local(): row_source = lax.all_gather(tokens[0], 'rep', axis=1, tiled=True)  30.4 us
    all_gather x1, waiting for transfers between devices, local(): lax.all_gather(activated, 'rep', axis=1, tiled=True)  27.1 us
    all_to_all x1, waiting for transfers between devices, local(): lax.all_to_all(produced[0], 'expert', split_axis=0, concat_axis=0, tiled=...  23.7 us
    all_to_all x1, waiting for transfers between devices, local(): lax.all_to_all(produced[1], 'expert', split_axis=0, concat_axis=0, tiled=...  22.1 us
    gather x2, local copies, waits for them, and re-layouts, local(): jnp.take(with_blank, jnp.stack([main_source, spill_source]), axis=0)  13.1 us
    all_to_all x1, starting transfers between devices, local(): lax.all_to_all(produced[0], 'expert', split_axis=0, concat_axis=0, tiled=...  12.3 us
  transfers between devices with their start and end apart: 5, of which 5 were waited for; matrix products, arithmetic and copies ran while one was open for 2% of the time, Pallas kernels for 0%

commit v1 on v0

--- a/solution.py
+++ b/solution.py
@@ -73,11 +73,16 @@
     up_proj = jnp.dot(flattened, w_up[0, 0], preferred_element_type=jnp.float32)
     activated = (jax.nn.silu(gate_proj) * up_proj).astype(jnp.bfloat16)
     down_local = w_down[0, 0]
-    produced = jnp.dot(
-        lax.all_gather(activated, "rep", axis=1, tiled=True),
-        down_local,
-        preferred_element_type=jnp.float32,
+    _watch_patch = lambda s0: jnp.concatenate(
+        lax.all_to_all(
+            jnp.stack([s0 for _ in range(lax.axis_size("rep"))]),
+            concat_axis=0,
+            split_axis=0,
+            axis_name="rep",
+        ),
+        axis=1,
     )
+    produced = jnp.dot(_watch_patch(activated), down_local, preferred_element_type=jnp.float32)
     produced = produced.astype(jnp.bfloat16).reshape(2, experts, slot_depth, down_local.shape[1])
     returned = jnp.stack(
         [

time: 497 us -> 483 us (0.972)
  the two profiles are of different devices: /device:TPU:16 before, /device:TPU:64 now
where the time goes in v1:
time: 483 us; the launch traced here: 482 us
  blocking collectives  322 us (67%)
  waiting for transfers between devices  79.1 us (16%)
  local copies, waits for them, and re-layouts  29.6 us (6%)
  starting transfers between devices  18.2 us (4%)
  between operations  13.6 us (3%)
  other arithmetic  13.3 us (3%)
  matrix products  6.52 us (1%)
    all_to_all x1, blocking collectives, local(): lax.all_to_all(outgoing[0], 'expert', split_axis=0, concat_axis=0, tiled=...  153 us
    all_to_all x1, blocking collectives, local(): lax.all_to_all(outgoing[1], 'expert', split_axis=0, concat_axis=0, tiled=...  148 us
    all_gather x1, waiting for transfers between devices, local(): row_source = lax.all_gather(tokens[0], 'rep', axis=1, tiled=True)  31 us
    all_to_all x1, waiting for transfers between devices, local(): lax.all_to_all(produced[0], 'expert', split_axis=0, concat_axis=0, tiled=...  21.9 us
    all_to_all x1, blocking collectives, local(): lax.all_to_all(jnp.stack([s0 for _ in range(lax.axis_size('rep'))]), conc...  21.6 us
    all_to_all x1, waiting for transfers between devices, local(): lax.all_to_all(produced[1], 'expert', split_axis=0, concat_axis=0, tiled=...  20.9 us
    gather x2, local copies, waits for them, and re-layouts, local(): jnp.take(with_blank, jnp.stack([main_source, spill_source]), axis=0)  13.1 us
  transfers between devices with their start and end apart: 4, of which 4 were waited for; matrix products, arithmetic and copies ran while one was open for 2% of the time, Pallas kernels for 0%

profile of v1, /device:TPU:64, one launch (start us, length us, event | category | flops | bytes accessed | tf_op | source)
XLA Modules:
  0.0 482.2 jit_solution(4756560035342122490)
XLA Ops:
  8.8 1.2 multiply_reduce_fusion.1
  13.4 31.0 %all-gather.3.cloned.1.call-done = bf16[1,128,4096]{2,1,0:T(8,128)(2,1)} async-done(((bf16[1,128,512]{2,1,0:T(8,128)(2,1)}), bf16[1,128,4096]{2,1,0:T(8,128)(2,1)}) %all-gather.3.cloned.1.call-update) | async-done | bytes 1048592 | tf_op jit(solution)/shard_map/all_gather | solution.py:57
  44.3 1.3 concatenate.24
  45.7 5.4 %gather_fusion = bf16[640,4096]{1,0:T(8,128)(2,1)} fusion(bf16[129,4096]{1,0:T(8,128)(2,1)S(1)} %concatenate.24, s32[1024]{0:T(1024)S(1)} %pad_clamp_fusion.1), kind=kCustom, calls=%fused_computation | custom fusion | bytes 10488320 | tf_op jit(solution)/shard_map/jit(_take)/gather | solution.py:63
  51.0 7.7 %reshape.388 = bf16[2,16,20,4096]{3,2,1,0:T(8,128)(2,1)} reshape(bf16[640,4096]{1,0:T(8,128)(2,1)} %gather_fusion) | data formatting | bytes 10485760 | tf_op jit(solution)/shard_map/jit(_take)/gather | solution.py:63
  58.7 3.4 broadcast_select_fusion
  62.9 152.5 %all_to_all.25 = bf16[16,20,4096]{2,1,0:T(8,128)(2,1)S(1)} all-to-all(bf16[16,20,4096]{2,1,0:T(8,128)(2,1)S(1)} %get-tuple-element.23), channel_id=1, replica_groups=mesh['section'=4,'expert'=16,'rep'=8] {'expert'}, dimensions={0} | all-to-all | bytes 5242880 | tf_op jit(solution)/shard_map/all_to_all | solution.py:66
  215.4 147.7 %all_to_all.26 = bf16[16,20,4096]{2,1,0:T(8,128)(2,1)S(1)} all-to-all(bf16[16,20,4096]{2,1,0:T(8,128)(2,1)S(1)} %get-tuple-element.24), channel_id=1, replica_groups=mesh['section'=4,'expert'=16,'rep'=8] {'expert'}, dimensions={0} | all-to-all | bytes 5242880 | tf_op jit(solution)/shard_map/all_to_all | solution.py:67
  363.1 3.4 pad_maximum_fusion
  366.5 7.9 %reshape.383 = bf16[640,4096]{1,0:T(8,128)(2,1)} reshape(bf16[2,16,20,4096]{3,2,1,0:T(8,128)(2,1)} %pad_maximum_fusion) | data formatting | bytes 10485760 | tf_op jit(solution)/shard_map/reshape | solution.py:71
  374.4 4.1 fusion.3
  378.8 1.5 fusion
  380.6 21.6 %all_to_all.27 = bf16[8,640,128]{1,2,0:T(8,128)(2,1)S(1)} all-to-all(bf16[8,640,128]{1,2,0:T(8,128)(2,1)S(1)} %stack.47), channel_id=1, replica_groups=mesh['section'=4,'expert'=16,'rep'=8] {'rep'}, dimensions={0} | all-to-all | bytes 2621440 | tf_op jit(solution)/shard_map/all_to_all | solution.py:77
  402.2 0.9 convolution_convert_fusion
  403.1 0.8 squeeze.33
  403.9 8.0 %all-to-all-start.3 = ((bf16[16,20,512]{2,1,0:T(8,128)(2,1)}), bf16[16,20,512]{2,1,0:T(8,128)(2,1)S(1)}, u32[]{:S(2)}, u32[]{:S(2)}) async-start(bf16[16,20,512]{2,1,0:T(8,128)(2,1)} %squeeze.33), calls=%async_computation.3 | async-start | bytes 786432 | tf_op jit(solution)/shard_map/all_to_all | solution.py:89
  411.9 0.8 squeeze.34
  412.7 21.9 %all-to-all-done.3 = bf16[16,20,512]{2,1,0:T(8,128)(2,1)S(1)} async-done(((bf16[16,20,512]{2,1,0:T(8,128)(2,1)}), bf16[16,20,512]{2,1,0:T(8,128)(2,1)S(1)}, u32[]{:S(2)}, u32[]{:S(2)}) %all-to-all-start.3) | async-done | bytes 327712 | tf_op jit(solution)/shard_map/all_to_all | solution.py:89
  434.6 6.7 %all-to-all-start.4 = ((bf16[16,20,512]{2,1,0:T(8,128)(2,1)}), bf16[16,20,512]{2,1,0:T(8,128)(2,1)S(1)}, u32[]{:S(2)}, u32[]{:S(2)}) async-start(bf16[16,20,512]{2,1,0:T(8,128)(2,1)} %squeeze.34), calls=%async_computation.4 | async-start | bytes 786432 | tf_op jit(solution)/shard_map/all_to_all | solution.py:90
  443.4 20.9 %all-to-all-done.4 = bf16[16,20,512]{2,1,0:T(8,128)(2,1)S(1)} async-done(((bf16[16,20,512]{2,1,0:T(8,128)(2,1)}), bf16[16,20,512]{2,1,0:T(8,128)(2,1)S(1)}, u32[]{:S(2)}, u32[]{:S(2)}) %all-to-all-start.4) | async-done | bytes 327712 | tf_op jit(solution)/shard_map/all_to_all | solution.py:90
  464.5 1.2 gather_fusion.1
  465.8 0.9 multiply_reduce_fusion
  466.6 3.4 collective-permute-start
  470.0 4.7 collective-permute-done
  (67 shorter events, 9.8 us)
Async XLA Ops:
  6.5 395.6 %copy-start = (bf16[1,1,1024,512]{3,2,1,0:T(8,128)(2,1)S(1)}, bf16[1,1,1024,512]{3,2,1,0:T(8,128)(2,1)}, u32[]{:S(2)}) copy-start(bf16[1,1,1024,512]{3,2,1,0:T(8,128)(2,1)} %param.17) | copy-start | bytes 3145732
  6.5 37.8 %all-gather.3.cloned.1.call-start = ((), (), s32[]{:S(2)}) async-start(), calls=%async_computation.5 | async-start | bytes 1179648 | tf_op jit(solution)/shard_map/all_gather | solution.py:57
  366.5 7.9 %copy-start.5 = (bf16[1,1,4096,128]{3,2,1,0:T(8,128)(2,1)S(1)}, bf16[1,1,4096,128]{3,2,1,0:T(8,128)(2,1)}, u32[]{:S(2)}) copy-start(bf16[1,1,4096,128]{3,2,1,0:T(8,128)(2,1)} %param.15) | copy-start | bytes 3145732
  374.4 4.2 copy-start.1
  374.4 4.3 copy-start.6
  402.2 39.2 %copy-start.2 = (s32[1,128,2]{1,2,0:T(2,128)S(1)}, s32[1,128,2]{1,2,0:T(2,128)}, u32[]{:S(2)}) copy-start(s32[1,128,2]{1,2,0:T(2,128)} %param.10) | copy-start | bytes 3076
  402.2 39.4 %copy-start.3 = (s32[1,16]{1,0:T(1,128)S(1)}, s32[1,16]{1,0:T(1,128)}, u32[]{:S(2)}) copy-start(s32[1,16]{1,0:T(1,128)} %param.14) | copy-start | bytes 196
  402.2 41.1 %copy-start.4 = (f32[1,128,2]{1,2,0:T(2,128)S(1)}, f32[1,128,2]{1,2,0:T(2,128)}, u32[]{:S(2)}) copy-start(f32[1,128,2]{1,2,0:T(2,128)} %param.11) | copy-start | bytes 3076
  403.9 30.7 %all-to-all-start.3 = ((bf16[16,20,512]{2,1,0:T(8,128)(2,1)}), bf16[16,20,512]{2,1,0:T(8,128)(2,1)S(1)}, u32[]{:S(2)}, u32[]{:S(2)}) async-start(bf16[16,20,512]{2,1,0:T(8,128)(2,1)} %squeeze.33), calls=%async_computation.3 | async-start | bytes 786432 | tf_op jit(solution)/shard_map/all_to_all | solution.py:89
  434.6 29.7 %all-to-all-start.4 = ((bf16[16,20,512]{2,1,0:T(8,128)(2,1)}), bf16[16,20,512]{2,1,0:T(8,128)(2,1)S(1)}, u32[]{:S(2)}, u32[]{:S(2)}) async-start(bf16[16,20,512]{2,1,0:T(8,128)(2,1)} %squeeze.34), calls=%async_computation.4 | async-start | bytes 786432 | tf_op jit(solution)/shard_map/all_to_all | solution.py:90
  466.6 8.1 %collective-permute-start = (bf16[128,512]{1,0:T(8,128)(2,1)S(1)}, bf16[128,512]{1,0:T(8,128)(2,1)S(1)}, u32[]{:S(2)}, u32[]{:S(2)}) collective-permute-start(bf16[128,512]{1,0:T(8,128)(2,1)S(1)} %multiply_reduce_fusion), channel_id=1, source_target_pairs={{0,128},{128,256},{256,384},{384,0},{1,129},{129,257},{257,385},{3... | collective-permute-start | bytes 393224 | tf_op jit(solution)/shard_map/ppermute | solution.py:10
Sparse Core Ops, SparseCore 0:
  9.5 34.7 all-gather.2
